TPU v7x, 32 devices: a whole 2x2x4 slice. The times are simulated.
32 devices in a mesh: dp: 8 (over z, core), mp: 4 (over y, x).
Axes of the slice: x: 2, y: 2, z: 4, core: 2. Of those that a mesh axis runs over, the one named last changes fastest.
Arguments:
- tokens: bfloat16 [16, 640, 2048], P('dp', 'mp'), may hold values from -6 to 6
- lengths: int32 [16], P('dp'), may hold values from 320 to 640, as said below
- w_query: bfloat16 [2048, 2048], P(None, 'mp'), may hold values from -0.125 to 0.125
- w_key: bfloat16 [2048, 2048], P(None, 'mp'), may hold values from -0.125 to 0.125
- w_value: bfloat16 [2048, 2048], P(None, 'mp'), may hold values from -0.125 to 0.125
- b_query: float32 [16, 128], P('mp'), may hold values from -3 to 3
- b_value: float32 [16, 128], P('mp'), may hold values from -2 to 2
- w_out: bfloat16 [2048, 2048], P('mp'), may hold values from -1 to 1
- b_out: float32 [2048], replicated, may hold values from -2 to 2
- w_up: bfloat16 [2048, 8192], P(None, 'mp'), may hold values from -0.125 to 0.125
- b_up: float32 [64, 128], P('mp'), may hold values from -2 to 2
- w_down: bfloat16 [8192, 2048], P('mp'), may hold values from -0.0625 to 0.0625
- b_down: float32 [2048], replicated, may hold values from -2 to 2
- norm1_gain: float32 [2048], replicated, may hold values from 0.5 to 1.5
- norm1_shift: float32 [2048], replicated, may hold values from -1.5 to 1.5
- norm2_gain: float32 [2048], replicated, may hold values from 0.5 to 1.5
- norm2_shift: float32 [2048], replicated, may hold values from -1.5 to 1.5
- cotangent: bfloat16 [16, 640, 2048], P('dp', 'mp'), may hold values from -6 to 6
Outputs:
- output: bfloat16 [16, 640, 2048], P('dp', 'mp')
- grad_tokens: bfloat16 [16, 640, 2048], P('dp', 'mp')
- grad_w_query: float32 [2048, 2048], P('dp', 'mp')
- grad_w_key: float32 [2048, 2048], P('dp', 'mp')
- grad_w_value: float32 [2048, 2048], P('dp', 'mp')
- grad_b_query: float32 [16, 128], P('mp', 'dp')
- grad_b_value: float32 [16, 128], P('mp', 'dp')
- grad_w_out: float32 [2048, 2048], P('mp', 'dp')
- grad_b_out: float32 [2048], P(('dp', 'mp'))
- grad_w_up: float32 [2048, 8192], P('dp', 'mp')
- grad_b_up: float32 [64, 128], P('mp', 'dp')
- grad_w_down: float32 [8192, 2048], P('mp', 'dp')
- grad_b_down: float32 [2048], P(('dp', 'mp'))
- grad_norm1_gain: float32 [2048], P(('dp', 'mp'))
- grad_norm1_shift: float32 [2048], P(('dp', 'mp'))
- grad_norm2_gain: float32 [2048], P(('dp', 'mp'))
- grad_norm2_shift: float32 [2048], P(('dp', 'mp'))
Inputs may be any that keep to these rules, and one draw needn't show every extreme that they name: `lengths`: each item has 320 to 640 valid slots, the first ones; some item is full.
All inputs are finite; a program needn't handle non-finite values.
Results may differ from a plain program's by a relative error of at most 0.02.
Values may be sent and summed in bfloat16 or wider, within the bound.
No kernel may reach another device: no remote copies, remote signals or barrier semaphores. Data moves between devices by JAX's collectives and lax.ppermute only.
A program may use at most 256 MiB of HBM per device.

v0:
```python
from functools import partial

import jax
import jax.numpy as jnp
from jax import lax
from jax.sharding import PartitionSpec as P

HEAD_DIM = 128


def layer_norm(values, gain, shift):
    centre = values - jnp.mean(values, axis=-1, keepdims=True)
    spread = jnp.mean(centre * centre, axis=-1, keepdims=True)
    return centre * lax.rsqrt(spread + 1e-05) * gain + shift


def allowed_keys(lengths, seq_len):
    places = jnp.arange(seq_len)
    causal = places[None, :] <= places[:, None]
    inside = places[None, None, :] < lengths[:, None, None]
    return (causal[None] & inside)[:, None]


def head_scores(query_heads, key_heads, allowed):
    scores = jnp.einsum(
        "iqhd,ikhd->ihqk", query_heads, key_heads, preferred_element_type=jnp.float32
    ) * HEAD_DIM ** (-0.5)
    return jnp.where(allowed, scores, -1e30)


def body(
    tokens,
    lengths,
    w_query,
    w_key,
    w_value,
    b_query,
    b_value,
    w_out,
    b_out,
    w_up,
    b_up,
    w_down,
    b_down,
    norm1_gain,
    norm1_shift,
    norm2_gain,
    norm2_shift,
    cotangent,
):
    f32 = jnp.float32
    bf16 = jnp.bfloat16
    rows_in = tokens.astype(f32)
    normed_one = layer_norm(rows_in, norm1_gain, norm1_shift).astype(bf16)
    full_one = lax.all_gather(normed_one, "mp", axis=1, tiled=True)
    items, seq_len = (full_one.shape[0], full_one.shape[1])
    heads_here = w_query.shape[1] // HEAD_DIM
    split = (items, seq_len, heads_here, HEAD_DIM)

    def project(weight):
        return jnp.einsum("isd,de->ise", full_one, weight, preferred_element_type=f32)

    queries = (project(w_query) + b_query.reshape(-1)).astype(bf16)
    keys_all = project(w_key).astype(bf16)
    values_all = (project(w_value) + b_value.reshape(-1)).astype(bf16)
    query_heads = queries.reshape(split)
    key_heads = keys_all.reshape(split)
    value_heads = values_all.reshape(split)
    allowed = allowed_keys(lengths, seq_len)
    scores = head_scores(query_heads, key_heads, allowed)
    row_max = jnp.max(scores, axis=-1, keepdims=True)
    raw_weights = jnp.exp(scores - row_max)
    row_total = jnp.sum(raw_weights, axis=-1, keepdims=True)
    probs = (raw_weights / row_total).astype(bf16)
    mixed = (
        jnp.einsum("ihqk,ikhd->iqhd", probs, value_heads, preferred_element_type=f32)
        .reshape(items, seq_len, -1)
        .astype(bf16)
    )
    attn_terms = jnp.einsum("ise,ed->isd", mixed, w_out, preferred_element_type=f32)
    attn_rows = lax.psum_scatter(
        attn_terms.astype(jnp.bfloat16), "mp", scatter_dimension=1, tiled=True
    ).astype(jnp.float32)
    middle = rows_in + attn_rows + b_out
    normed_two = layer_norm(middle, norm2_gain, norm2_shift).astype(bf16)
    full_two = lax.all_gather(normed_two, "mp", axis=1, tiled=True)
    hidden_pre = jnp.einsum(
        "isd,df->isf", full_two, w_up, preferred_element_type=f32
    ) + b_up.reshape(-1)
    hidden = jax.nn.gelu(hidden_pre, approximate=False).astype(bf16)
    ffn_terms = jnp.einsum("isf,fd->isd", hidden, w_down, preferred_element_type=f32)
    ffn_rows = lax.psum_scatter(
        ffn_terms.astype(jnp.bfloat16), "mp", scatter_dimension=1, tiled=True
    ).astype(jnp.float32)
    result = (middle + ffn_rows + b_down).astype(bf16)
    grad_out = cotangent.astype(f32)
    grad_full = lax.all_gather(cotangent, "mp", axis=1, tiled=True)
    grad_w_down = jnp.einsum("isf,isd->fd", hidden, grad_full, preferred_element_type=f32)
    grad_b_down = jnp.sum(grad_out, axis=(0, 1))
    grad_hidden = jnp.einsum("isd,fd->isf", grad_full, w_down, preferred_element_type=f32)
    _, gelu_back = jax.vjp(partial(jax.nn.gelu, approximate=False), hidden_pre)
    grad_pre = gelu_back(grad_hidden)[0].astype(bf16)
    grad_w_up = jnp.einsum("isd,isf->df", full_two, grad_pre, preferred_element_type=f32)
    grad_b_up = jnp.sum(grad_pre, axis=(0, 1), dtype=f32).reshape(b_up.shape)
    back_terms = jnp.einsum("isf,df->isd", grad_pre, w_up, preferred_element_type=f32)
    back_rows = lax.psum_scatter(
        back_terms.astype(jnp.bfloat16), "mp", scatter_dimension=1, tiled=True
    ).astype(jnp.float32)
    _, second_back = jax.vjp(layer_norm, middle, norm2_gain, norm2_shift)
    grad_mid_norm, grad_gain_two, grad_shift_two = second_back(back_rows)
    grad_middle = grad_out + grad_mid_norm
    grad_b_out = jnp.sum(grad_middle, axis=(0, 1))
    middle_full = lax.all_gather(grad_middle.astype(bf16), "mp", axis=1, tiled=True)
    grad_w_out = jnp.einsum("ise,isd->ed", mixed, middle_full, preferred_element_type=f32)
    grad_mixed = (
        jnp.einsum("isd,ed->ise", middle_full, w_out, preferred_element_type=f32)
        .astype(bf16)
        .reshape(split)
    )
    again = head_scores(query_heads, key_heads, allowed)
    probs_full = jnp.exp(again - row_max) / row_total
    probs_low = probs_full.astype(bf16)
    grad_value = (
        jnp.einsum("ihqk,iqhd->ikhd", probs_low, grad_mixed, preferred_element_type=f32)
        .astype(bf16)
        .reshape(items, seq_len, -1)
    )
    grad_probs = jnp.einsum("iqhd,ikhd->ihqk", grad_mixed, value_heads, preferred_element_type=f32)
    inner = jnp.sum(probs_full * grad_probs, axis=-1, keepdims=True)
    grad_scores = (probs_full * (grad_probs - inner)).astype(bf16)
    grad_query = (
        (
            jnp.einsum("ihqk,ikhd->iqhd", grad_scores, key_heads, preferred_element_type=f32)
            * HEAD_DIM ** (-0.5)
        )
        .astype(bf16)
        .reshape(items, seq_len, -1)
    )
    grad_key = (
        (
            jnp.einsum("ihqk,iqhd->ikhd", grad_scores, query_heads, preferred_element_type=f32)
            * HEAD_DIM ** (-0.5)
        )
        .astype(bf16)
        .reshape(items, seq_len, -1)
    )

    def weight_grad(grad_cols):
        return jnp.einsum("isd,ise->de", full_one, grad_cols, preferred_element_type=f32)

    grad_w_query = weight_grad(grad_query)
    grad_w_key = weight_grad(grad_key)
    grad_w_value = weight_grad(grad_value)
    grad_b_query = jnp.sum(grad_query, axis=(0, 1), dtype=f32).reshape(b_query.shape)
    grad_b_value = jnp.sum(grad_value, axis=(0, 1), dtype=f32).reshape(b_value.shape)
    back_one = (
        jnp.einsum("ise,de->isd", grad_query, w_query, preferred_element_type=f32)
        + jnp.einsum("ise,de->isd", grad_key, w_key, preferred_element_type=f32)
        + jnp.einsum("ise,de->isd", grad_value, w_value, preferred_element_type=f32)
    )
    rows_one = lax.psum_scatter(
        back_one.astype(jnp.bfloat16), "mp", scatter_dimension=1, tiled=True
    ).astype(jnp.float32)
    _, first_back = jax.vjp(layer_norm, rows_in, norm1_gain, norm1_shift)
    grad_in_norm, grad_gain_one, grad_shift_one = first_back(rows_one)
    grad_inputs = (grad_middle + grad_in_norm).astype(bf16)
    every_sum = (
        lax.psum_scatter(
            grad_w_query.astype(jnp.bfloat16), "dp", scatter_dimension=0, tiled=True
        ).astype(jnp.float32),
        lax.psum_scatter(
            grad_w_key.astype(jnp.bfloat16), "dp", scatter_dimension=0, tiled=True
        ).astype(jnp.float32),
        lax.psum_scatter(
            grad_w_value.astype(jnp.bfloat16), "dp", scatter_dimension=0, tiled=True
        ).astype(jnp.float32),
        lax.psum_scatter(
            grad_b_query.astype(jnp.bfloat16), "dp", scatter_dimension=1, tiled=True
        ).astype(jnp.float32),
        lax.psum_scatter(
            grad_b_value.astype(jnp.bfloat16), "dp", scatter_dimension=1, tiled=True
        ).astype(jnp.float32),
        lax.psum_scatter(
            grad_w_out.astype(jnp.bfloat16), "dp", scatter_dimension=1, tiled=True
        ).astype(jnp.float32),
        lax.psum_scatter(
            grad_w_up.astype(jnp.bfloat16), "dp", scatter_dimension=0, tiled=True
        ).astype(jnp.float32),
        lax.psum_scatter(
            grad_w_down.astype(jnp.bfloat16), "dp", scatter_dimension=1, tiled=True
        ).astype(jnp.float32),
        lax.psum_scatter(
            grad_b_up.astype(jnp.bfloat16), "dp", scatter_dimension=1, tiled=True
        ).astype(jnp.float32),
    )
    (
        sum_w_query,
        sum_w_key,
        sum_w_value,
        sum_b_query,
        sum_b_value,
        sum_w_out,
        sum_w_up,
        sum_w_down,
        sum_b_up,
    ) = every_sum
    vector_sums = (
        lax.psum_scatter(grad_b_out, ("dp", "mp"), scatter_dimension=0, tiled=True),
        lax.psum_scatter(grad_b_down, ("dp", "mp"), scatter_dimension=0, tiled=True),
        lax.psum_scatter(grad_gain_one, ("dp", "mp"), scatter_dimension=0, tiled=True),
        lax.psum_scatter(grad_shift_one, ("dp", "mp"), scatter_dimension=0, tiled=True),
        lax.psum_scatter(grad_gain_two, ("dp", "mp"), scatter_dimension=0, tiled=True),
        lax.psum_scatter(grad_shift_two, ("dp", "mp"), scatter_dimension=0, tiled=True),
    )
    sum_b_out, sum_b_down, sum_gain_one, sum_shift_one, sum_gain_two, sum_shift_two = vector_sums
    return (
        result,
        grad_inputs,
        sum_w_query,
        sum_w_key,
        sum_w_value,
        sum_b_query,
        sum_b_value,
        sum_w_out,
        sum_b_out,
        sum_w_up,
        sum_b_up,
        sum_w_down,
        sum_b_down,
        sum_gain_one,
        sum_shift_one,
        sum_gain_two,
        sum_shift_two,
    )


def solution(mesh):
    return jax.shard_map(
        body,
        mesh=mesh,
        in_specs=(
            P("dp", "mp", None),
            P("dp"),
            P(None, "mp"),
            P(None, "mp"),
            P(None, "mp"),
            P("mp", None),
            P("mp", None),
            P("mp", None),
            P(),
            P(None, "mp"),
            P("mp", None),
            P("mp", None),
            P(),
            P(),
            P(),
            P(),
            P(),
            P("dp", "mp", None),
        ),
        out_specs=(
            P("dp", "mp", None),
            P("dp", "mp", None),
            P("dp", "mp"),
            P("dp", "mp"),
            P("dp", "mp"),
            P("mp", "dp"),
            P("mp", "dp"),
            P("mp", "dp"),
            P(("dp", "mp")),
            P("dp", "mp"),
            P("mp", "dp"),
            P("mp", "dp"),
            P(("dp", "mp")),
            P(("dp", "mp")),
            P(("dp", "mp")),
            P(("dp", "mp")),
            P(("dp", "mp")),
        ),
        check_vma=False,
    )
```

profile of v0, /device:TPU:0, one launch (start us, length us, event | category | flops | bytes accessed | tf_op | source)
XLA Modules:
  0.0 1041.9 jit_solution(1776042553797564077)
XLA Ops:
  15.3 62.6 %all-gather.5.cloned.1.call-done = bf16[2,640,2048]{2,1,0:T(8,128)(2,1)} async-done(((bf16[2,160,2048]{2,1,0:T(8,128)(2,1)}), bf16[2,640,2048]{2,1,0:T(8,128)(2,1)}) %all-gather.5.cloned.1.call-update) | async-done | bytes 5242896 | tf_op jit(solution)/shard_map/all_gather | solution.py:55
  77.8 7.3 fusion.66
  85.1 4.3 add_convert_fusion.5
  89.4 11.4 %fusion.92 = (f32[2,4,640]{2,1,0:T(4,128)S(1)}, f32[2,4,640,640]{2,3,1,0:T(8,128)}) fusion(pred[2,640,640]{1,2,0:T(8,128)(4,1)} %broadcast_and_fusion, bf16[2,640,4,128]{1,3,2,0:T(8,128)(2,1)} %bitcast.133, bf16[2,640,4,128]{1,3,2,0:T(8,128)(2,1)} %bitcast.127), kind=kOutput, calls=%fused_computation.134 | convolution fusion | flops 851968640 | bytes 16568320 | tf_op jit(solution)/shard_map/sub | solution.py:72
  100.8 6.5 add_convert_fusion.6
  110.2 4.7 convolution_convert_fusion
  115.0 61.4 %reduce-scatter.20.cloned.1.call-done = bf16[2,160,2048]{2,1,0:T(8,128)(2,1)} async-done(((bf16[2,640,2048]{2,1,0:T(8,128)(2,1)}), bf16[2,160,2048]{2,1,0:T(8,128)(2,1)}) %reduce-scatter.20.cloned.1.call-update) | async-done | bytes 1310736 | tf_op jit(solution)/shard_map/reduce_scatter | solution.py:81
  182.0 60.4 %all-gather.7.cloned.1.call-done = bf16[2,640,2048]{2,1,0:T(8,128)(2,1)} async-done(((bf16[2,160,2048]{2,1,0:T(8,128)(2,1)}), bf16[2,640,2048]{2,1,0:T(8,128)(2,1)}) %all-gather.7.cloned.1.call-update) | async-done | bytes 5242896 | tf_op jit(solution)/shard_map/all_gather | solution.py:86
  242.5 20.1 %fusion.48 = (u8[640,2048]{1,0:T(8,128)(4,1)}, u8[640,2048]{1,0:T(8,128)(4,1)}, f32[2,640,2048]{2,1,0:T(8,128)S(1)}) fusion(f32[2048]{0:T(1024)S(1)} %bitcast.140, bf16[2,640,2048]{2,1,0:T(8,128)(2,1)} %all-gather.7.cloned.1.call-done, bf16[2048,2048]{1,0:T(8,128)(2,1)} %param.27), kind=kOutput, calls=%fused_computation.91 | convolution fusion | flops 10771496960 | bytes 26746880 | tf_op jit(solution)/shard_map/isd,df->isf/dot_general | solution.py:87
  262.5 3.9 copy-done.13
  266.4 26.6 %multiply_convert_fusion.1 = (bf16[2,640,2048]{2,1,0:T(8,128)(2,1)}, f32[2,640,2048]{2,1,0:T(8,128)}) fusion(f32[2,640,2048]{2,1,0:T(8,128)S(1)} %get-tuple-element.41, f32[2048]{0:T(1024)S(1)} %bitcast.141, u8[640,2048]{1,0:T(8,128)(4,1)} %get-tuple-element.18, u8[640,2048]{1,0:T(8,128)(4,1)} %get-tuple-element.17), kind=kLoop, calls=%fused_computation.16 | loop fusion | flops 186122240 | bytes 28844032 | tf_op jit(solution)/shard_map/convert_element_type | solution.py:90
  293.0 12.5 %all-gather.9.cloned.1.call-done = bf16[2,640,2048]{2,1,0:T(8,128)(2,1)} async-done(((bf16[2,160,2048]{2,1,0:T(8,128)(2,1)}), bf16[2,640,2048]{2,1,0:T(8,128)(2,1)}) %all-gather.9.cloned.1.call-update) | async-done | bytes 5242896 | tf_op jit(solution)/shard_map/all_gather | solution.py:97
  305.5 25.0 %fusion.93 = (bf16[2048]{0:T(1024)(128)(2,1)S(1)}, bf16[2,640,2048]{2,1,0:T(8,128)(2,1)}) fusion(f32[2,640,2048]{2,1,0:T(8,128)} %get-tuple-element.36, bf16[2,640,2048]{2,1,0:T(8,128)(2,1)} %all-gather.9.cloned.1.call-done, bf16[2048,2048]{1,0:T(8,128)(2,1)} %param.29, f32[2,640,2048]{2,1,0:T(8,128)} %copy-done.13, f32[2048]{0:T(1024)S(1)} %bitcast.142), kind=kOutput, calls=%fused_computation.135 | convolution fusion | flops 10779359232 | bytes 39858176 | tf_op jit(solution)/shard_map/isd,fd->isf/dot_general | solution.py:100
  330.5 16.6 %fusion.21 = bf16[2,640,2048]{2,1,0:T(8,128)(2,1)} fusion(bf16[2,640,2048]{2,1,0:T(8,128)(2,1)} %get-tuple-element.49, bf16[2048,2048]{1,0:T(8,128)(2,1)} %param.27), kind=kOutput, calls=%fused_computation.46 | convolution fusion | flops 10740039680 | bytes 18874368 | tf_op jit(solution)/shard_map/isf,df->isd/dot_general | solution.py:105
  347.4 61.2 %reduce-scatter.24.cloned.1.call-done = bf16[2,160,2048]{2,1,0:T(8,128)(2,1)} async-done(((bf16[2,640,2048]{2,1,0:T(8,128)(2,1)}), bf16[2,160,2048]{2,1,0:T(8,128)(2,1)}) %reduce-scatter.24.cloned.1.call-update) | async-done | bytes 1310736 | tf_op jit(solution)/shard_map/reduce_scatter | solution.py:106
  408.6 3.5 convert_reduce_fusion.1
  413.9 2.4 fusion.90
  417.2 16.7 %bitcast_convert_fusion.1 = bf16[2048,2048]{1,0:T(8,128)(2,1)} fusion(bf16[2,640,2048]{2,1,0:T(8,128)(2,1)} %all-gather.7.cloned.1.call-done, bf16[2,640,2048]{2,1,0:T(8,128)(2,1)} %get-tuple-element.49), kind=kOutput, calls=%fused_computation.2 | convolution fusion | flops 10741612544 | bytes 18874368 | tf_op jit(solution)/shard_map/isd,isf->df/dot_general | solution.py:103
  434.4 16.7 %bitcast_convert_fusion = bf16[2048,2048]{1,0:T(8,128)(2,1)} fusion(bf16[2,640,2048]{2,1,0:T(8,128)(2,1)} %get-tuple-element.35, bf16[2,640,2048]{2,1,0:T(8,128)(2,1)} %all-gather.9.cloned.1.call-done), kind=kOutput, calls=%fused_computation.1 | convolution fusion | flops 10741612544 | bytes 18874368 | tf_op jit(solution)/shard_map/isf,isd->fd/dot_general | solution.py:98
  451.1 26.6 %all-gather.11.cloned.1.call-done = bf16[2,640,2048]{2,1,0:T(8,128)(2,1)} async-done(((bf16[2,160,2048]{2,1,0:T(8,128)(2,1)}), bf16[2,640,2048]{2,1,0:T(8,128)(2,1)}) %all-gather.11.cloned.1.call-update) | async-done | bytes 5242896 | tf_op jit(solution)/shard_map/all_gather | solution.py:113
  477.8 5.4 fusion.69
  483.2 8.1 bitcast_reduce_fusion
  492.0 8.7 multiply_reduce_fusion
  501.0 9.5 multiply_convert_fusion
  514.1 7.2 bitcast_convert_fusion.2
  521.4 6.8 bitcast_convert_fusion.3
  528.2 6.7 bitcast_convert_fusion.5
  536.3 4.9 multiply_convert_fusion.2
  542.3 6.9 bitcast_convert_fusion.4
  549.3 7.0 fusion.52
  556.3 5.5 fusion.56
  561.8 11.4 %add_convert_fusion = bf16[2,640,2048]{2,1,0:T(8,128)(2,1)} fusion(f32[2,640,2048]{2,1,0:T(8,128)} %fusion.56, f32[2,640,2048]{2,1,0:T(8,128)} %fusion.52, bf16[2,640,512]{1,2,0:T(8,128)(2,1)S(1)} %bitcast.132, bf16[2048,512]{1,0:T(8,128)(2,1)S(1)} %copy-done.15), kind=kOutput, calls=%fused_computation.14 | convolution fusion | flops 2692218880 | bytes 29622272 | tf_op jit(solution)/shard_map/ise,de->isd/dot_general | solution.py:159
  573.5 16.6 %fusion.24 = bf16[2,640,2048]{2,1,0:T(8,128)(2,1)} fusion(bf16[2,640,2048]{2,1,0:T(8,128)(2,1)} %get-tuple-element.35, bf16[2048,2048]{1,0:T(8,128)(2,1)} %param.29), kind=kOutput, calls=%fused_computation.47 | convolution fusion | flops 10740039680 | bytes 18874368 | tf_op jit(solution)/shard_map/isf,fd->isd/dot_general | solution.py:91
  591.6 9.5 reduce-scatter.36.cloned.1.call-done
  601.1 2.8 convert_element_type.196
  603.9 87.5 %reduce-scatter.38.cloned.1.call-done = bf16[2048,256]{1,0:T(8,128)(2,1)} async-done(((bf16[2048,2048]{1,0:T(8,128)(2,1)}), bf16[2048,256]{1,0:T(8,128)(2,1)}) %reduce-scatter.38.cloned.1.call-update) | async-done | bytes 1048592 | tf_op jit(solution)/shard_map/reduce_scatter | solution.py:189
  691.4 2.7 convert_element_type.200
  694.1 29.0 %reduce-scatter.42.cloned.1.call-done = bf16[16,4]{1,0:T(8,128)(2,1)} async-done(((bf16[128,4]{1,0:T(8,128)(2,1)}), bf16[16,4]{1,0:T(8,128)(2,1)}) %reduce-scatter.42.cloned.1.call-update) | async-done | bytes 144
  724.4 30.1 %reduce-scatter.40.cloned.1.call-done = bf16[16,4]{1,0:T(8,128)(2,1)} async-done(((bf16[128,4]{1,0:T(8,128)(2,1)}), bf16[16,4]{1,0:T(8,128)(2,1)}) %reduce-scatter.40.cloned.1.call-update) | async-done | bytes 144
  755.9 34.9 %reduce-scatter.34.cloned.1.call-done = bf16[512,256]{1,0:T(8,128)(2,1)} async-done(((bf16[512,2048]{1,0:T(8,128)(2,1)}), bf16[512,256]{1,0:T(8,128)(2,1)}) %reduce-scatter.34.cloned.1.call-update) | async-done | bytes 262160 | tf_op jit(solution)/shard_map/reduce_scatter | solution.py:183
  792.6 35.1 %reduce-scatter.32.cloned.1.call-done = bf16[256,512]{1,0:T(8,128)(2,1)} async-done(((bf16[2048,512]{1,0:T(8,128)(2,1)}), bf16[256,512]{1,0:T(8,128)(2,1)}) %reduce-scatter.32.cloned.1.call-update) | async-done | bytes 262160 | tf_op jit(solution)/shard_map/reduce_scatter | solution.py:174
  829.5 35.1 %reduce-scatter.28.cloned.1.call-done = bf16[256,512]{1,0:T(8,128)(2,1)} async-done(((bf16[2048,512]{1,0:T(8,128)(2,1)}), bf16[256,512]{1,0:T(8,128)(2,1)}) %reduce-scatter.28.cloned.1.call-update) | async-done | bytes 262160 | tf_op jit(solution)/shard_map/reduce_scatter | solution.py:168
  866.4 35.0 %reduce-scatter.30.cloned.1.call-done = bf16[256,512]{1,0:T(8,128)(2,1)} async-done(((bf16[2048,512]{1,0:T(8,128)(2,1)}), bf16[256,512]{1,0:T(8,128)(2,1)}) %reduce-scatter.30.cloned.1.call-update) | async-done | bytes 262160 | tf_op jit(solution)/shard_map/reduce_scatter | solution.py:171
  903.2 61.0 %reduce-scatter.26.cloned.1.call-done = bf16[2,160,2048]{2,1,0:T(8,128)(2,1)} async-done(((bf16[2,640,2048]{2,1,0:T(8,128)(2,1)}), bf16[2,160,2048]{2,1,0:T(8,128)(2,1)}) %reduce-scatter.26.cloned.1.call-update) | async-done | bytes 1310736 | tf_op jit(solution)/shard_map/reduce_scatter | solution.py:161
  966.5 5.1 fusion.45
  971.7 40.7 %all-reduce.6 = (f32[2048]{0:T(1024)S(1)}, f32[2048]{0:T(1024)S(1)}, f32[2048]{0:T(1024)S(1)}, f32[2048]{0:T(1024)S(1)}, f32[2048]{0:T(1024)S(1)}, /*index=5*/f32[2048]{0:T(1024)S(1)}) all-reduce(f32[2048]{0:T(1024)S(1)} %get-tuple-element.20, f32[2048]{0:T(1024)S(1)} %get-tuple-element.23, ...), channel_id=12, replica_groups=mesh['dp'=8,'mp'=4] {'dp','mp'}, use_global_device_ids=true, to_apply=%region_24.25.clone | all-reduce | flops 12288 | bytes 98304
  1015.9 13.4 %reduce-scatter.22.cloned.1.call-done = bf16[2,160,2048]{2,1,0:T(8,128)(2,1)} async-done(((bf16[2,640,2048]{2,1,0:T(8,128)(2,1)}), bf16[2,160,2048]{2,1,0:T(8,128)(2,1)}) %reduce-scatter.22.cloned.1.call-update) | async-done | bytes 1310736 | tf_op jit(solution)/shard_map/reduce_scatter | solution.py:92
  1029.2 5.8 add_convert_fusion.2
  (184 shorter events, 44.2 us)
Async XLA Ops:
  7.2 103.0 %copy-start = (bf16[512,2048]{1,0:T(8,128)(2,1)S(1)}, bf16[512,2048]{1,0:T(8,128)(2,1)}, u32[]{:S(2)}) copy-start(bf16[512,2048]{1,0:T(8,128)(2,1)} %param.25) | copy-start | bytes 6291460
  7.2 70.6 %all-gather.5.cloned.1.call-start = ((), (), s32[]{:S(2)}) async-start(), calls=%async_computation.13 | async-start | bytes 6553600 | tf_op jit(solution)/shard_map/all_gather | solution.py:55
  13.7 162.7 %reduce-scatter.20.cloned.1.call-start = ((), (), s32[]{:S(2)}) async-start(), calls=%async_computation.14 | async-start | bytes 6553600 | tf_op jit(solution)/shard_map/reduce_scatter | solution.py:81
  15.3 69.9 %copy-start.50 = (f32[4,128]{1,0:T(4,128)S(1)}, f32[4,128]{1,0:T(4,128)}, u32[]{:S(2)}) copy-start(f32[4,128]{1,0:T(4,128)} %param.23) | copy-start | bytes 6148
  77.8 7.3 copy-start.46
  77.8 7.3 copy-start.48
  89.4 11.4 %copy-start.51 = (f32[4,128]{1,0:T(4,128)S(1)}, f32[4,128]{1,0:T(4,128)}, u32[]{:S(2)}) copy-start(f32[4,128]{1,0:T(4,128)} %param.24) | copy-start | bytes 6148
  100.8 6.9 copy-start.12
  114.9 61.5 %copy-start.20 = (f32[2048]{0:T(1024)S(1)}, f32[2048]{0:T(1024)}, u32[]{:S(2)}) copy-start(f32[2048]{0:T(1024)} %param.26) | copy-start | bytes 24580
  114.9 64.2 %copy-start.22 = (f32[2048]{0:T(1024)S(1)}, f32[2048]{0:T(1024)}, u32[]{:S(2)}) copy-start(f32[2048]{0:T(1024)} %param.33) | copy-start | bytes 24580
  114.9 64.2 %copy-start.42 = (f32[2048]{0:T(1024)S(1)}, f32[2048]{0:T(1024)}, u32[]{:S(2)}) copy-start(f32[2048]{0:T(1024)} %param.34) | copy-start | bytes 24580
  114.9 127.6 %all-gather.7.cloned.1.call-start = ((), (), s32[]{:S(2)}) async-start(), calls=%async_computation.15 | async-start | bytes 6553600 | tf_op jit(solution)/shard_map/all_gather | solution.py:86
  178.3 235.0 %copy-start.24 = (f32[2,160]{1,0:T(2,128)}, f32[2,160]{1,0:T(2,128)S(1)}, u32[]{:S(2)}) copy-start(f32[2,160]{1,0:T(2,128)S(1)} %broadcast_multiply_fusion) | copy-start | bytes 3844
  179.1 234.3 %copy-start.28 = (f32[2,160]{1,0:T(2,128)}, f32[2,160]{1,0:T(2,128)S(1)}, u32[]{:S(2)}) copy-start(f32[2,160]{1,0:T(2,128)S(1)} %fusion.86) | copy-start | bytes 3844
  179.1 63.4 %copy-start.44 = (f32[16,128]{1,0:T(8,128)S(1)}, f32[16,128]{1,0:T(8,128)}, u32[]{:S(2)}) copy-start(f32[16,128]{1,0:T(8,128)} %param.28) | copy-start | bytes 24580
  181.0 124.5 %all-gather.9.cloned.1.call-start = ((), (), s32[]{:S(2)}) async-start(), calls=%async_computation.17 | async-start | bytes 6553600 | tf_op jit(solution)/shard_map/all_gather | solution.py:97
  181.6 227.0 %reduce-scatter.24.cloned.1.call-start = ((), (), s32[]{:S(2)}) async-start(), calls=%async_computation.18 | async-start | bytes 6553600 | tf_op jit(solution)/shard_map/reduce_scatter | solution.py:106
  347.1 130.6 %all-gather.11.cloned.1.call-start = ((), (), s32[]{:S(2)}) async-start(), calls=%async_computation.19 | async-start | bytes 6553600 | tf_op jit(solution)/shard_map/all_gather | solution.py:113
  416.3 173.9 %reduce-scatter.44.cloned.1.call-start = ((), (), s32[]{:S(2)}) async-start(), calls=%async_computation.29 | async-start | bytes 36864
  417.1 184.0 %reduce-scatter.36.cloned.1.call-start = ((), (), s32[]{:S(2)}) async-start(), calls=%async_computation.25 | async-start | bytes 9437184 | tf_op jit(solution)/shard_map/reduce_scatter | solution.py:186
  433.9 257.5 %reduce-scatter.38.cloned.1.call-start = ((), (), s32[]{:S(2)}) async-start(), calls=%async_computation.26 | async-start | bytes 9437184 | tf_op jit(solution)/shard_map/reduce_scatter | solution.py:189
  451.1 272.0 %reduce-scatter.42.cloned.1.call-start = ((), (), s32[]{:S(2)}) async-start(), calls=%async_computation.28 | async-start | bytes 36864
  483.2 8.8 copy-start.54
  500.8 253.8 %reduce-scatter.40.cloned.1.call-start = ((), (), s32[]{:S(2)}) async-start(), calls=%async_computation.27 | async-start | bytes 36864
  501.0 9.6 copy-start.14
  514.0 7.3 copy-start.16
  514.0 276.8 %reduce-scatter.34.cloned.1.call-start = ((), (), s32[]{:S(2)}) async-start(), calls=%async_computation.24 | async-start | bytes 2359296 | tf_op jit(solution)/shard_map/reduce_scatter | solution.py:183
  521.3 306.4 %reduce-scatter.32.cloned.1.call-start = ((), (), s32[]{:S(2)}) async-start(), calls=%async_computation.23 | async-start | bytes 2359296 | tf_op jit(solution)/shard_map/reduce_scatter | solution.py:174
  528.2 336.4 %reduce-scatter.28.cloned.1.call-start = ((), (), s32[]{:S(2)}) async-start(), calls=%async_computation.21 | async-start | bytes 2359296 | tf_op jit(solution)/shard_map/reduce_scatter | solution.py:168
  535.0 366.4 %reduce-scatter.30.cloned.1.call-start = ((), (), s32[]{:S(2)}) async-start(), calls=%async_computation.22 | async-start | bytes 2359296 | tf_op jit(solution)/shard_map/reduce_scatter | solution.py:171
  542.3 7.0 copy-start.47
  549.2 415.0 %reduce-scatter.26.cloned.1.call-start = ((), (), s32[]{:S(2)}) async-start(), calls=%async_computation.20 | async-start | bytes 6553600 | tf_op jit(solution)/shard_map/reduce_scatter | solution.py:161
  549.3 7.0 copy-start.49
  573.2 456.0 %reduce-scatter.22.cloned.1.call-start = ((), (), s32[]{:S(2)}) async-start(), calls=%async_computation.16 | async-start | bytes 6553600 | tf_op jit(solution)/shard_map/reduce_scatter | solution.py:92
  603.9 360.4 %copy-start.3 = (bf16[2,160,2048]{2,1,0:T(8,128)(2,1)S(1)}, bf16[2,160,2048]{2,1,0:T(8,128)(2,1)}, u32[]{:S(2)}) copy-start(bf16[2,160,2048]{2,1,0:T(8,128)(2,1)} %param.18) | copy-start | bytes 3932164
  603.9 360.4 %copy-start.27 = (f32[2048]{0:T(1024)S(1)}, f32[2048]{0:T(1024)}, u32[]{:S(2)}) copy-start(f32[2048]{0:T(1024)} %param.31) | copy-start | bytes 24580
  603.9 360.4 %copy-start.31 = (f32[2,160]{1,0:T(2,128)S(1)}, f32[2,160]{1,0:T(2,128)}, u32[]{:S(2)}) copy-start(f32[2,160]{1,0:T(2,128)} %copy-done.30) | copy-start | bytes 3844
  792.6 173.8 %copy-start.40 = (f32[2,160]{1,0:T(2,128)S(1)}, f32[2,160]{1,0:T(2,128)}, u32[]{:S(2)}) copy-start(f32[2,160]{1,0:T(2,128)} %copy-done.39) | copy-start | bytes 3844
  792.6 173.8 %copy-start.6 = (bf16[2,160,2048]{2,1,0:T(8,128)(2,1)S(1)}, bf16[2,160,2048]{2,1,0:T(8,128)(2,1)}, u32[]{:S(2)}) copy-start(bf16[2,160,2048]{2,1,0:T(8,128)(2,1)} %reduce-scatter.20.cloned.1.call-done) | copy-start | bytes 3932164
  792.6 173.8 %copy-start.21 = (f32[2048]{0:T(1024)S(1)}, f32[2048]{0:T(1024)}, u32[]{:S(2)}) copy-start(f32[2048]{0:T(1024)} %param.26) | copy-start | bytes 24580
  792.6 173.8 %copy-start.23 = (f32[2048]{0:T(1024)S(1)}, f32[2048]{0:T(1024)}, u32[]{:S(2)}) copy-start(f32[2048]{0:T(1024)} %param.33) | copy-start | bytes 24580
  792.6 173.9 %copy-start.25 = (f32[2,160]{1,0:T(2,128)S(1)}, f32[2,160]{1,0:T(2,128)}, u32[]{:S(2)}) copy-start(f32[2,160]{1,0:T(2,128)} %copy-done.24) | copy-start | bytes 3844
  792.6 173.9 %copy-start.29 = (f32[2,160]{1,0:T(2,128)S(1)}, f32[2,160]{1,0:T(2,128)}, u32[]{:S(2)}) copy-start(f32[2,160]{1,0:T(2,128)} %copy-done.28) | copy-start | bytes 3844
  792.6 173.9 %copy-start.33 = (f32[2,160]{1,0:T(2,128)S(1)}, f32[2,160]{1,0:T(2,128)}, u32[]{:S(2)}) copy-start(f32[2,160]{1,0:T(2,128)} %copy-done.32) | copy-start | bytes 3844
  792.6 173.9 %copy-start.35 = (f32[2,160]{1,0:T(2,128)S(1)}, f32[2,160]{1,0:T(2,128)}, u32[]{:S(2)}) copy-start(f32[2,160]{1,0:T(2,128)} %copy-done.34) | copy-start | bytes 3844
  792.6 173.9 %copy-start.37 = (f32[2,160]{1,0:T(2,128)S(1)}, f32[2,160]{1,0:T(2,128)}, u32[]{:S(2)}) copy-start(f32[2,160]{1,0:T(2,128)} %copy-done.36) | copy-start | bytes 3844
  966.5 62.7 %copy-start.43 = (f32[2048]{0:T(1024)S(1)}, f32[2048]{0:T(1024)}, u32[]{:S(2)}) copy-start(f32[2048]{0:T(1024)} %param.30) | copy-start | bytes 24580
  1029.2 5.8 copy-start.1
  (24 other events, 68.0 us)
Sparse Core Ops, SparseCore 0:
  13.8 64.0 all-gather.4
  115.0 61.3 reduce-scatter.19
  181.1 61.3 all-gather.6
  244.2 61.2 all-gather.8
  347.2 61.3 reduce-scatter.23
  416.4 61.2 all-gather.10
  480.6 30.4 reduce-scatter.43
  513.4 87.6 reduce-scatter.35
  603.4 87.9 reduce-scatter.37
  694.1 28.9 reduce-scatter.41
  725.9 28.5 reduce-scatter.39
  756.7 34.0 reduce-scatter.33
  793.1 34.5 reduce-scatter.31
  829.9 34.6 reduce-scatter.27
  866.7 34.6 reduce-scatter.29
  904.3 59.9 reduce-scatter.25
  967.1 62.1 reduce-scatter.21
where the time goes:
time: 1050 us; the launch traced here: 1040 us
  waiting for transfers between devices  656 us (62%)
  matrix products  227 us (22%)
  other arithmetic  81.9 us (8%)
  blocking collectives  40.7 us (4%)
  local copies, waits for them, and re-layouts  18.7 us (2%)
  between operations  15 us (1%)
    reduce_scatter x1, waiting for transfers between devices, body(): lax.psum_scatter(grad_w_down.astype(jnp.bfloat16), 'dp', scatter_dimensio...  87.5 us
    all_gather x1, waiting for transfers between devices, body(): full_one = lax.all_gather(normed_one, 'mp', axis=1, tiled=True)  62.6 us
    reduce_scatter x1, waiting for transfers between devices, body(): lax.psum_scatter(attn_terms.astype(jnp.bfloat16), 'mp', scatter_dimension...  61.4 us
    reduce_scatter x1, waiting for transfers between devices, body(): lax.psum_scatter(back_terms.astype(jnp.bfloat16), 'mp', scatter_dimension...  61.2 us
    reduce_scatter x1, waiting for transfers between devices, body(): lax.psum_scatter(back_one.astype(jnp.bfloat16), 'mp', scatter_dimension=1...  61 us
    all_gather x1, waiting for transfers between devices, body(): full_two = lax.all_gather(normed_two, 'mp', axis=1, tiled=True)  60.4 us
    unnamed x20, waiting for transfers between devices  59.9 us
    unnamed x1, blocking collectives  40.7 us
  transfers between devices with their start and end apart: 17, of which 16 were waited for; matrix products, arithmetic and copies ran while one was open for 21% of the time, Pallas kernels for 0%

commit v1 on v0

--- a/solution.py
+++ b/solution.py
@@ -6,6 +6,59 @@
 from jax.sharding import PartitionSpec as P
 
 HEAD_DIM = 128
+
+
+def _pairs(n, flip):
+    return [(m, m ^ flip) for m in range(n)]
+
+
+def gather_rows(x, axis=1):
+    n = lax.axis_size("mp")
+    if n != 4:
+        return lax.all_gather(x, "mp", axis=axis, tiled=True)
+    me = lax.axis_index("mp")
+    rows = x.shape[axis]
+    half = rows // 2
+    from_x = lax.ppermute(x, "mp", _pairs(n, 1))
+    from_y = lax.ppermute(x, "mp", _pairs(n, 2))
+    diag_a = lax.ppermute(lax.slice_in_dim(from_y, 0, half, axis=axis), "mp", _pairs(n, 1))
+    diag_b = lax.ppermute(lax.slice_in_dim(from_x, half, rows, axis=axis), "mp", _pairs(n, 2))
+    diag = jnp.concatenate([diag_a, diag_b], axis=axis)
+    shape = list(x.shape)
+    shape[axis] = rows * n
+    full = jnp.zeros(shape, x.dtype)
+    for flip, piece in ((0, x), (1, from_x), (2, from_y), (3, diag)):
+        start = [0] * x.ndim
+        start[axis] = (me ^ flip) * rows
+        full = lax.dynamic_update_slice(full, piece, start)
+    return full
+
+
+def scatter_rows(y, axis=1):
+    n = lax.axis_size("mp")
+    if n != 4:
+        return lax.psum_scatter(
+            y.astype(jnp.bfloat16), "mp", scatter_dimension=axis, tiled=True
+        ).astype(jnp.float32)
+    me = lax.axis_index("mp")
+    rows = y.shape[axis] // n
+    half = rows // 2
+
+    def part(flip, lo, hi):
+        return lax.dynamic_slice_in_dim(y, (me ^ flip) * rows + lo, hi - lo, axis=axis)
+
+    bf16 = jnp.bfloat16
+    send_x = jnp.stack([part(1, 0, half), part(3, 0, half)]).astype(bf16)
+    send_y = jnp.stack([part(2, half, rows), part(3, half, rows)]).astype(bf16)
+    got_x = lax.ppermute(send_x, "mp", _pairs(n, 1))
+    got_y = lax.ppermute(send_y, "mp", _pairs(n, 2))
+    fwd_y = (got_x[1].astype(jnp.float32) + part(2, 0, half)).astype(bf16)
+    fwd_x = (got_y[1].astype(jnp.float32) + part(1, half, rows)).astype(bf16)
+    last_y = lax.ppermute(fwd_y, "mp", _pairs(n, 2))
+    last_x = lax.ppermute(fwd_x, "mp", _pairs(n, 1))
+    low = part(0, 0, half) + got_x[0].astype(jnp.float32) + last_y.astype(jnp.float32)
+    high = part(0, half, rows) + got_y[0].astype(jnp.float32) + last_x.astype(jnp.float32)
+    return jnp.concatenate([low, high], axis=axis)
 
 
 def layer_norm(values, gain, shift):
@@ -52,7 +105,7 @@
     bf16 = jnp.bfloat16
     rows_in = tokens.astype(f32)
     normed_one = layer_norm(rows_in, norm1_gain, norm1_shift).astype(bf16)
-    full_one = lax.all_gather(normed_one, "mp", axis=1, tiled=True)
+    full_one = gather_rows(normed_one)
     items, seq_len = (full_one.shape[0], full_one.shape[1])
     heads_here = w_query.shape[1] // HEAD_DIM
     split = (items, seq_len, heads_here, HEAD_DIM)
@@ -78,23 +131,19 @@
         .astype(bf16)
     )
     attn_terms = jnp.einsum("ise,ed->isd", mixed, w_out, preferred_element_type=f32)
-    attn_rows = lax.psum_scatter(
-        attn_terms.astype(jnp.bfloat16), "mp", scatter_dimension=1, tiled=True
-    ).astype(jnp.float32)
+    attn_rows = scatter_rows(attn_terms)
     middle = rows_in + attn_rows + b_out
     normed_two = layer_norm(middle, norm2_gain, norm2_shift).astype(bf16)
-    full_two = lax.all_gather(normed_two, "mp", axis=1, tiled=True)
+    full_two = gather_rows(normed_two)
     hidden_pre = jnp.einsum(
         "isd,df->isf", full_two, w_up, preferred_element_type=f32
     ) + b_up.reshape(-1)
     hidden = jax.nn.gelu(hidden_pre, approximate=False).astype(bf16)
     ffn_terms = jnp.einsum("isf,fd->isd", hidden, w_down, preferred_element_type=f32)
-    ffn_rows = lax.psum_scatter(
-        ffn_terms.astype(jnp.bfloat16), "mp", scatter_dimension=1, tiled=True
-    ).astype(jnp.float32)
+    ffn_rows = scatter_rows(ffn_terms)
     result = (middle + ffn_rows + b_down).astype(bf16)
     grad_out = cotangent.astype(f32)
-    grad_full = lax.all_gather(cotangent, "mp", axis=1, tiled=True)
+    grad_full = gather_rows(cotangent)
     grad_w_down = jnp.einsum("isf,isd->fd", hidden, grad_full, preferred_element_type=f32)
     grad_b_down = jnp.sum(grad_out, axis=(0, 1))
     grad_hidden = jnp.einsum("isd,fd->isf", grad_full, w_down, preferred_element_type=f32)
@@ -103,14 +152,12 @@
     grad_w_up = jnp.einsum("isd,isf->df", full_two, grad_pre, preferred_element_type=f32)
     grad_b_up = jnp.sum(grad_pre, axis=(0, 1), dtype=f32).reshape(b_up.shape)
     back_terms = jnp.einsum("isf,df->isd", grad_pre, w_up, preferred_element_type=f32)
-    back_rows = lax.psum_scatter(
-        back_terms.astype(jnp.bfloat16), "mp", scatter_dimension=1, tiled=True
-    ).astype(jnp.float32)
+    back_rows = scatter_rows(back_terms)
     _, second_back = jax.vjp(layer_norm, middle, norm2_gain, norm2_shift)
     grad_mid_norm, grad_gain_two, grad_shift_two = second_back(back_rows)
     grad_middle = grad_out + grad_mid_norm
     grad_b_out = jnp.sum(grad_middle, axis=(0, 1))
-    middle_full = lax.all_gather(grad_middle.astype(bf16), "mp", axis=1, tiled=True)
+    middle_full = gather_rows(grad_middle.astype(bf16))
     grad_w_out = jnp.einsum("ise,isd->ed", mixed, middle_full, preferred_element_type=f32)
     grad_mixed = (
         jnp.einsum("isd,ed->ise", middle_full, w_out, preferred_element_type=f32)
@@ -158,9 +205,7 @@
         + jnp.einsum("ise,de->isd", grad_key, w_key, preferred_element_type=f32)
         + jnp.einsum("ise,de->isd", grad_value, w_value, preferred_element_type=f32)
     )
-    rows_one = lax.psum_scatter(
-        back_one.astype(jnp.bfloat16), "mp", scatter_dimension=1, tiled=True
-    ).astype(jnp.float32)
+    rows_one = scatter_rows(back_one)
     _, first_back = jax.vjp(layer_norm, rows_in, norm1_gain, norm1_shift)
     grad_in_norm, grad_gain_one, grad_shift_one = first_back(rows_one)
     grad_inputs = (grad_middle + grad_in_norm).astype(bf16)

time: 1050 us -> 962 us (0.916)
  waiting for transfers between devices: 656 us -> 488 us
  local copies, waits for them, and re-layouts: 18.7 us -> 53.1 us
  starting transfers between devices: 2.11 us -> 33 us
  other arithmetic: 81.9 us -> 95.5 us
    ppermute x0 -> x32, waiting for transfers between devices: none -> 316 us  [the longest x4 97.3 us: scatter_rows(): got_x = lax.ppermute(send_x, 'mp', _pairs(n, 1))]
    reduce_scatter x4 -> x0, waiting for transfers between devices: 197 us -> none  [the longest x1 61.4 us: body(): lax.psum_scatter(attn_terms.astype(jnp.bfloat16), 'mp', scatter_dimension...]
    all_gather x4 -> x0, waiting for transfers between devices: 162 us -> none  [the longest x1 62.6 us: body(): full_one = lax.all_gather(normed_one, 'mp', axis=1, tiled=True)]
    reduce_scatter x1, waiting for transfers between devices: 9.5 us -> 83.9 us  [body(): lax.psum_scatter(grad_w_up.astype(jnp.bfloat16), 'dp', scatter_dimension=...]
    unnamed x20 -> x12, waiting for transfers between devices: 59.9 us -> 0.17 us
    reduce_scatter x1, waiting for transfers between devices: 35.1 us -> 0.01 us  [body(): lax.psum_scatter(grad_w_value.astype(jnp.bfloat16), 'dp', scatter_dimensi...]
    reduce_scatter x1, waiting for transfers between devices: 35.1 us -> 0.01 us  [body(): lax.psum_scatter(grad_w_query.astype(jnp.bfloat16), 'dp', scatter_dimensi...]
    reduce_scatter x1, waiting for transfers between devices: 35 us -> 0.01 us  [body(): lax.psum_scatter(grad_w_key.astype(jnp.bfloat16), 'dp', scatter_dimension...]
  transfers between devices with their start and end apart: 17 -> 41, of which waited for: 16 -> 28; matrix products, arithmetic and copies ran while one was open for 21% -> 19% of each run, Pallas kernels for 0% -> 0%
where the time goes in v1:
time: 962 us; the launch traced here: 952 us
  waiting for transfers between devices  488 us (51%)
  matrix products  226 us (23%)
  other arithmetic  95.5 us (10%)
  local copies, waits for them, and re-layouts  53.1 us (6%)
  blocking collectives  41.6 us (4%)
  starting transfers between devices  33 us (3%)
  between operations  15.1 us (2%)
    ppermute x4, waiting for transfers between devices, scatter_rows(): got_x = lax.ppermute(send_x, 'mp', _pairs(n, 1))  97.3 us
    reduce_scatter x1, waiting for transfers between devices, body(): lax.psum_scatter(grad_w_down.astype(jnp.bfloat16), 'dp', scatter_dimensio...  87.5 us
    reduce_scatter x1, waiting for transfers between devices, body(): lax.psum_scatter(grad_w_up.astype(jnp.bfloat16), 'dp', scatter_dimension=...  83.9 us
    ppermute x4, waiting for transfers between devices, gather_rows(): from_x = lax.ppermute(x, 'mp', _pairs(n, 1))  82.8 us
    ppermute x4, waiting for transfers between devices, scatter_rows(): last_y = lax.ppermute(fwd_y, 'mp', _pairs(n, 2))  48.5 us
    unnamed x1, blocking collectives  41.6 us
    ppermute x4, waiting for transfers between devices, scatter_rows(): last_x = lax.ppermute(fwd_x, 'mp', _pairs(n, 1))  36.8 us
    unnamed x142, local copies, waits for them, and re-layouts  26.4 us
  transfers between devices with their start and end apart: 41, of which 28 were waited for; matrix products, arithmetic and copies ran while one was open for 19% of the time, Pallas kernels for 0%

profile of v1, /device:TPU:0, one launch (start us, length us, event | category | flops | bytes accessed | tf_op | source)
XLA Modules:
  0.0 951.6 jit_solution(5629968213466753242)
XLA Ops:
  20.8 27.1 %collective-permute-done = bf16[2,160,2048]{2,1,0:T(8,128)(2,1)S(1)} collective-permute-done((bf16[2,160,2048]{2,1,0:T(8,128)(2,1)S(1)}, bf16[2,160,2048]{2,1,0:T(8,128)(2,1)S(1)}, u32[]{:S(2)}, u32[]{:S(2)}) %collective-permute-start) | collective-permute-done | bytes 1310752 | tf_op jit(solution)/shard_map/ppermute | solution.py:22
  60.3 5.7 collective-permute-done.3
  71.7 6.7 fusion.56
  78.4 6.7 add_convert_fusion.3
  85.2 6.8 add_convert_fusion.4
  91.9 11.4 %fusion.127 = (f32[2,4,640]{2,1,0:T(4,128)S(1)}, f32[2,4,640,640]{2,3,1,0:T(8,128)}) fusion(pred[2,640,640]{1,2,0:T(8,128)(4,1)} %broadcast_and_fusion, bf16[2,640,4,128]{1,3,2,0:T(8,128)(2,1)} %bitcast.247, bf16[2,640,4,128]{1,3,2,0:T(8,128)(2,1)} %bitcast.241), kind=kOutput, calls=%fused_computation.235 | convolution fusion | flops 851968640 | bytes 16568320 | tf_op jit(solution)/shard_map/sub | solution.py:125
  103.3 6.6 fusion.62
  118.2 24.8 %collective-permute-done.4 = bf16[2,2,80,2048]{3,2,1,0:T(8,128)(2,1)S(1)} collective-permute-done((bf16[2,2,80,2048]{3,2,1,0:T(8,128)(2,1)S(1)}, bf16[2,2,80,2048]{3,2,1,0:T(8,128)(2,1)S(1)}, u32[]{:S(2)}, u32[]{:S(2)}) %collective-permute-start.4) | collective-permute-done | bytes 1310752 | tf_op jit(solution)/shard_map/ppermute | solution.py:53
  148.4 12.0 %collective-permute-done.5 = bf16[2,80,2048]{2,1,0:T(8,128)(2,1)} collective-permute-done((bf16[2,80,2048]{2,1,0:T(8,128)(2,1)}, bf16[2,80,2048]{2,1,0:T(8,128)(2,1)}, u32[]{:S(2)}, u32[]{:S(2)}) %collective-permute-start.5) | collective-permute-done | bytes 655392 | tf_op jit(solution)/shard_map/ppermute | solution.py:57
  160.4 4.0 fusion.87
  166.9 15.4 %collective-permute-done.7 = bf16[2,80,2048]{2,1,0:T(8,128)(2,1)} collective-permute-done((bf16[2,80,2048]{2,1,0:T(8,128)(2,1)}, bf16[2,80,2048]{2,1,0:T(8,128)(2,1)}, u32[]{:S(2)}, u32[]{:S(2)}) %collective-permute-start.7) | collective-permute-done | bytes 655392 | tf_op jit(solution)/shard_map/ppermute | solution.py:58
  188.6 8.1 collective-permute-done.17
  199.6 10.8 %collective-permute-done.16 = bf16[2,160,2048]{2,1,0:T(8,128)(2,1)} collective-permute-done((bf16[2,160,2048]{2,1,0:T(8,128)(2,1)}, bf16[2,160,2048]{2,1,0:T(8,128)(2,1)}, u32[]{:S(2)}, u32[]{:S(2)}) %collective-permute-start.16) | collective-permute-done | bytes 1310752 | tf_op jit(solution)/shard_map/ppermute | solution.py:22
  217.2 21.1 %collective-permute-done.8 = bf16[2,160,2048]{2,1,0:T(8,128)(2,1)S(1)} collective-permute-done((bf16[2,160,2048]{2,1,0:T(8,128)(2,1)S(1)}, bf16[2,160,2048]{2,1,0:T(8,128)(2,1)S(1)}, u32[]{:S(2)}, u32[]{:S(2)}) %collective-permute-start.8) | collective-permute-done | bytes 1310752 | tf_op jit(solution)/shard_map/ppermute | solution.py:22
  240.0 12.4 %collective-permute-done.18 = bf16[2,80,2048]{2,1,0:T(8,128)(2,1)S(1)} collective-permute-done((bf16[2,80,2048]{2,1,0:T(8,128)(2,1)S(1)}, bf16[2,80,2048]{2,1,0:T(8,128)(2,1)S(1)}, u32[]{:S(2)}, u32[]{:S(2)}) %collective-permute-start.18) | collective-permute-done | bytes 655392 | tf_op jit(solution)/shard_map/ppermute | solution.py:24
  255.0 8.6 collective-permute-done.10
  266.1 20.0 %fusion.40 = (u8[640,2048]{1,0:T(8,128)(4,1)S(1)}, u8[640,2048]{1,0:T(8,128)(4,1)}, f32[2,640,2048]{2,1,0:T(8,128)S(1)}) fusion(f32[2048]{0:T(1024)S(1)} %bitcast.254, bf16[2,640,2048]{2,1,0:T(8,128)(2,1)} %copy-done.14, bf16[2048,2048]{1,0:T(8,128)(2,1)} %param.27), kind=kOutput, calls=%fused_computation.84 | convolution fusion | flops 10771496960 | bytes 26746880 | tf_op jit(solution)/shard_map/isd,df->isf/dot_general | solution.py:138
  286.2 26.4 %multiply_convert_fusion.1 = (bf16[2,640,2048]{2,1,0:T(8,128)(2,1)S(1)}, f32[2,640,2048]{2,1,0:T(8,128)}) fusion(f32[2,640,2048]{2,1,0:T(8,128)S(1)} %get-tuple-element.77, f32[2048]{0:T(1024)S(1)} %bitcast.255, u8[640,2048]{1,0:T(8,128)(4,1)} %get-tuple-element.18, u8[640,2048]{1,0:T(8,128)(4,1)S(1)} %get-tuple-element.17), kind=kLoop, calls=%fused_computation.16 | loop fusion | flops 186122240 | bytes 28844032 | tf_op jit(solution)/shard_map/convert_element_type | solution.py:141
  312.6 17.8 %fusion.10 = f32[2,640,2048]{2,1,0:T(8,128)} fusion(bf16[2,640,2048]{2,1,0:T(8,128)(2,1)S(1)} %get-tuple-element.43, bf16[2048,2048]{1,0:T(8,128)(2,1)} %param.29), kind=kOutput, calls=%fused_computation.32 | convolution fusion | flops 10737418240 | bytes 24117248 | tf_op jit(solution)/shard_map/isf,fd->isd/dot_general | solution.py:142
  330.4 24.8 %fusion.128 = (bf16[2048]{0:T(1024)(128)(2,1)S(1)}, bf16[2,640,2048]{2,1,0:T(8,128)(2,1)}) fusion(f32[2,640,2048]{2,1,0:T(8,128)} %get-tuple-element.44, bf16[2,640,2048]{2,1,0:T(8,128)(2,1)} %copy-done.15, bf16[2048,2048]{1,0:T(8,128)(2,1)} %param.29, f32[2,640,2048]{2,1,0:T(8,128)} %copy-done.10, f32[2048]{0:T(1024)S(1)} %bitcast.256), kind=kOutput, calls=%fused_computation.236 | convolution fusion | flops 10779359232 | bytes 39858176 | tf_op jit(solution)/shard_map/isd,fd->isf/dot_general | solution.py:149
  355.2 17.9 %fusion.12 = f32[2,640,2048]{2,1,0:T(8,128)} fusion(bf16[2,640,2048]{2,1,0:T(8,128)(2,1)} %get-tuple-element.85, bf16[2048,2048]{1,0:T(8,128)(2,1)} %param.27), kind=kOutput, calls=%fused_computation.34 | convolution fusion | flops 10737418240 | bytes 24117248 | tf_op jit(solution)/shard_map/isf,df->isd/dot_general | solution.py:154
  381.2 26.6 %collective-permute-done.20 = bf16[2,2,80,2048]{3,2,1,0:T(8,128)(2,1)S(1)} collective-permute-done((bf16[2,2,80,2048]{3,2,1,0:T(8,128)(2,1)S(1)}, bf16[2,2,80,2048]{3,2,1,0:T(8,128)(2,1)S(1)}, u32[]{:S(2)}, u32[]{:S(2)}) %collective-permute-start.20) | collective-permute-done | bytes 1310752 | tf_op jit(solution)/shard_map/ppermute | solution.py:53
  409.7 22.4 %collective-permute-done.12 = bf16[2,2,80,2048]{3,2,1,0:T(8,128)(2,1)S(1)} collective-permute-done((bf16[2,2,80,2048]{3,2,1,0:T(8,128)(2,1)S(1)}, bf16[2,2,80,2048]{3,2,1,0:T(8,128)(2,1)S(1)}, u32[]{:S(2)}, u32[]{:S(2)}) %collective-permute-start.12) | collective-permute-done | bytes 1310752 | tf_op jit(solution)/shard_map/ppermute | solution.py:53
  432.6 20.1 %collective-permute-done.21 = bf16[2,80,2048]{2,1,0:T(8,128)(2,1)S(1)} collective-permute-done((bf16[2,80,2048]{2,1,0:T(8,128)(2,1)S(1)}, bf16[2,80,2048]{2,1,0:T(8,128)(2,1)S(1)}, u32[]{:S(2)}, u32[]{:S(2)}) %collective-permute-start.21) | collective-permute-done | bytes 655392 | tf_op jit(solution)/shard_map/ppermute | solution.py:57
  455.8 6.6 collective-permute-done.13
  463.3 7.5 collective-permute-done.23
  474.5 5.7 collective-permute-done.15
  488.0 23.8 %collective-permute-done.24 = bf16[2,160,2048]{2,1,0:T(8,128)(2,1)S(1)} collective-permute-done((bf16[2,160,2048]{2,1,0:T(8,128)(2,1)S(1)}, bf16[2,160,2048]{2,1,0:T(8,128)(2,1)S(1)}, u32[]{:S(2)}, u32[]{:S(2)}) %collective-permute-start.24) | collective-permute-done | bytes 1310752 | tf_op jit(solution)/shard_map/ppermute | solution.py:22
  530.0 5.6 fusion.59
  538.9 5.8 multiply_reduce_fusion
  545.5 9.5 multiply_convert_fusion
  558.6 7.3 bitcast_convert_fusion.2
  566.0 6.8 bitcast_convert_fusion.3
  573.0 6.7 bitcast_convert_fusion.5
  581.0 4.9 multiply_convert_fusion.2
  587.0 6.7 bitcast_convert_fusion.4
  593.9 16.7 %bitcast_convert_fusion.1 = bf16[2048,2048]{1,0:T(8,128)(2,1)} fusion(bf16[2,640,2048]{2,1,0:T(8,128)(2,1)} %copy-done.14, bf16[2,640,2048]{2,1,0:T(8,128)(2,1)} %get-tuple-element.85), kind=kOutput, calls=%fused_computation.2 | convolution fusion | flops 10741612544 | bytes 18874368 | tf_op jit(solution)/shard_map/isd,isf->df/dot_general | solution.py:152
  610.9 16.7 %bitcast_convert_fusion = bf16[2048,2048]{1,0:T(8,128)(2,1)} fusion(bf16[2,640,2048]{2,1,0:T(8,128)(2,1)} %copy-done.16, bf16[2,640,2048]{2,1,0:T(8,128)(2,1)} %copy-done.15), kind=kOutput, calls=%fused_computation.1 | convolution fusion | flops 10741612544 | bytes 18874368 | tf_op jit(solution)/shard_map/isf,isd->fd/dot_general | solution.py:147
  628.9 7.3 fusion.45
  636.2 5.7 fusion.49
  641.8 9.2 add_add_fusion
  654.1 23.5 %collective-permute-done.28 = bf16[2,2,80,2048]{3,2,1,0:T(8,128)(2,1)S(1)} collective-permute-done((bf16[2,2,80,2048]{3,2,1,0:T(8,128)(2,1)S(1)}, bf16[2,2,80,2048]{3,2,1,0:T(8,128)(2,1)S(1)}, u32[]{:S(2)}, u32[]{:S(2)}) %collective-permute-start.28) | collective-permute-done | bytes 1310752 | tf_op jit(solution)/shard_map/ppermute | solution.py:53
  678.3 5.2 collective-permute-done.30
  683.6 9.7 %collective-permute-done.29 = bf16[2,80,2048]{2,1,0:T(8,128)(2,1)S(1)} collective-permute-done((bf16[2,80,2048]{2,1,0:T(8,128)(2,1)S(1)}, bf16[2,80,2048]{2,1,0:T(8,128)(2,1)S(1)}, u32[]{:S(2)}, u32[]{:S(2)}) %collective-permute-start.29) | collective-permute-done | bytes 655392 | tf_op jit(solution)/shard_map/ppermute | solution.py:57
  699.2 8.2 collective-permute-done.31
  715.4 41.6 %all-reduce.6 = (f32[2048]{0:T(1024)S(1)}, f32[2048]{0:T(1024)S(1)}, f32[2048]{0:T(1024)S(1)}, f32[2048]{0:T(1024)S(1)}, f32[2048]{0:T(1024)S(1)}, /*index=5*/f32[2048]{0:T(1024)S(1)}) all-reduce(f32[2048]{0:T(1024)S(1)} %get-tuple-element.24, f32[2048]{0:T(1024)S(1)} %get-tuple-element.23, ...), channel_id=8, replica_groups=mesh['dp'=8,'mp'=4] {'dp','mp'}, use_global_device_ids=true, to_apply=%region_20.21.clone | all-reduce | flops 12288 | bytes 98304
  767.8 83.9 %reduce-scatter.24.cloned.1.call-done = bf16[256,2048]{1,0:T(8,128)(2,1)} async-done(((bf16[2048,2048]{1,0:T(8,128)(2,1)}), bf16[256,2048]{1,0:T(8,128)(2,1)}) %reduce-scatter.24.cloned.1.call-update) | async-done | bytes 1048592 | tf_op jit(solution)/shard_map/reduce_scatter | solution.py:231
  854.4 87.5 %reduce-scatter.26.cloned.1.call-done = bf16[2048,256]{1,0:T(8,128)(2,1)} async-done(((bf16[2048,2048]{1,0:T(8,128)(2,1)}), bf16[2048,256]{1,0:T(8,128)(2,1)}) %reduce-scatter.26.cloned.1.call-update) | async-done | bytes 1048592 | tf_op jit(solution)/shard_map/reduce_scatter | solution.py:234
  (296 shorter events, 160.1 us)
Async XLA Ops:
  7.2 103.7 %copy-start = (bf16[512,2048]{1,0:T(8,128)(2,1)S(1)}, bf16[512,2048]{1,0:T(8,128)(2,1)}, u32[]{:S(2)}) copy-start(bf16[512,2048]{1,0:T(8,128)(2,1)} %param.25) | copy-start | bytes 6291460
  7.2 687.8 %reduce-scatter.32.cloned.1.call-start = ((), (), s32[]{:S(2)}) async-start(), calls=%async_computation.17 | async-start | bytes 36864
  16.1 31.8 %collective-permute-start = (bf16[2,160,2048]{2,1,0:T(8,128)(2,1)S(1)}, bf16[2,160,2048]{2,1,0:T(8,128)(2,1)S(1)}, u32[]{:S(2)}, u32[]{:S(2)}) collective-permute-start(bf16[2,160,2048]{2,1,0:T(8,128)(2,1)S(1)} %get-tuple-element.50), channel_id=1, source_target_pairs={{0,1},{1,0},{2,3},{3,2},{4,5},{5,4},{6,7},{7,6},{8,9},{9,8},{10,11... | collective-permute-start | bytes 3932168 | tf_op jit(solution)/shard_map/ppermute | solution.py:22
  19.1 32.5 %collective-permute-start.1 = (bf16[2,160,2048]{2,1,0:T(8,128)(2,1)S(1)}, bf16[2,160,2048]{2,1,0:T(8,128)(2,1)S(1)}, u32[]{:S(2)}, u32[]{:S(2)}) collective-permute-start(bf16[2,160,2048]{2,1,0:T(8,128)(2,1)S(1)} %get-tuple-element.50), channel_id=1, source_target_pairs={{0,2},{1,3},{2,0},{3,1},{4,6},{5,7},{6,4},{7,5},{8,10},{9,11},{10,... | collective-permute-start | bytes 3932168 | tf_op jit(solution)/shard_map/ppermute | solution.py:23
  49.8 16.2 %collective-permute-start.3 = (bf16[2,80,2048]{2,1,0:T(8,128)(2,1)}, bf16[2,80,2048]{2,1,0:T(8,128)(2,1)}, u32[]{:S(2)}, u32[]{:S(2)}) collective-permute-start(bf16[2,80,2048]{2,1,0:T(8,128)(2,1)} %slice.97), channel_id=1, source_target_pairs={{0,2},{1,3},{2,0},{3,1},{4,6},{5,7},{6,4},{7,5},{8,10},{9,11},{10,... | collective-permute-start | bytes 1966088 | tf_op jit(solution)/shard_map/ppermute | solution.py:25
  53.5 15.7 %collective-permute-start.2 = (bf16[2,80,2048]{2,1,0:T(8,128)(2,1)}, bf16[2,80,2048]{2,1,0:T(8,128)(2,1)}, u32[]{:S(2)}, u32[]{:S(2)}) collective-permute-start(bf16[2,80,2048]{2,1,0:T(8,128)(2,1)} %slice.96), channel_id=1, source_target_pairs={{0,1},{1,0},{2,3},{3,2},{4,5},{5,4},{6,7},{7,6},{8,9},{9,8},{10,11... | collective-permute-start | bytes 1966088 | tf_op jit(solution)/shard_map/ppermute | solution.py:24
  113.9 29.1 %copy-start.12 = (f32[2,640,2048]{2,1,0:T(8,128)}, f32[2,640,2048]{2,1,0:T(8,128)S(1)}, u32[]{:S(2)}) copy-start(f32[2,640,2048]{2,1,0:T(8,128)S(1)} %fusion.43) | copy-start | bytes 31457284
  114.4 28.6 %collective-permute-start.4 = (bf16[2,2,80,2048]{3,2,1,0:T(8,128)(2,1)S(1)}, bf16[2,2,80,2048]{3,2,1,0:T(8,128)(2,1)S(1)}, u32[]{:S(2)}, u32[]{:S(2)}) collective-permute-start(bf16[2,2,80,2048]{3,2,1,0:T(8,128)(2,1)S(1)} %pad_maximum_fusion.2), channel_id=1, source_target_pairs={{0,1},{1,0},{2,3},{3,2},{4,5},{5,4},{6,7},{7,6},{8,9},{9,8},{10,11... | collective-permute-start | bytes 3932168 | tf_op jit(solution)/shard_map/ppermute | solution.py:53
  117.7 30.7 %collective-permute-start.6 = (bf16[2,2,80,2048]{3,2,1,0:T(8,128)(2,1)}, bf16[2,2,80,2048]{3,2,1,0:T(8,128)(2,1)}, u32[]{:S(2)}, u32[]{:S(2)}) collective-permute-start(bf16[2,2,80,2048]{3,2,1,0:T(8,128)(2,1)} %pad_maximum_fusion.3), channel_id=1, source_target_pairs={{0,2},{1,3},{2,0},{3,1},{4,6},{5,7},{6,4},{7,5},{8,10},{9,11},{10,... | collective-permute-start | bytes 3932168 | tf_op jit(solution)/shard_map/ppermute | solution.py:54
  144.3 16.1 %collective-permute-start.5 = (bf16[2,80,2048]{2,1,0:T(8,128)(2,1)}, bf16[2,80,2048]{2,1,0:T(8,128)(2,1)}, u32[]{:S(2)}, u32[]{:S(2)}) collective-permute-start(bf16[2,80,2048]{2,1,0:T(8,128)(2,1)} %fusion.86), channel_id=1, source_target_pairs={{0,2},{1,3},{2,0},{3,1},{4,6},{5,7},{6,4},{7,5},{8,10},{9,11},{10,... | collective-permute-start | bytes 1966088 | tf_op jit(solution)/shard_map/ppermute | solution.py:57
  164.4 17.9 %collective-permute-start.7 = (bf16[2,80,2048]{2,1,0:T(8,128)(2,1)}, bf16[2,80,2048]{2,1,0:T(8,128)(2,1)}, u32[]{:S(2)}, u32[]{:S(2)}) collective-permute-start(bf16[2,80,2048]{2,1,0:T(8,128)(2,1)} %get-tuple-element.68), channel_id=1, source_target_pairs={{0,1},{1,0},{2,3},{3,2},{4,5},{5,4},{6,7},{7,6},{8,9},{9,8},{10,11... | collective-permute-start | bytes 1966088 | tf_op jit(solution)/shard_map/ppermute | solution.py:58
  164.7 32.0 %collective-permute-start.17 = (bf16[2,160,2048]{2,1,0:T(8,128)(2,1)}, bf16[2,160,2048]{2,1,0:T(8,128)(2,1)}, u32[]{:S(2)}, u32[]{:S(2)}) collective-permute-start(bf16[2,160,2048]{2,1,0:T(8,128)(2,1)} %param.35), channel_id=1, source_target_pairs={{0,2},{1,3},{2,0},{3,1},{4,6},{5,7},{6,4},{7,5},{8,10},{9,11},{10,... | collective-permute-start | bytes 3932168 | tf_op jit(solution)/shard_map/ppermute | solution.py:23
  165.8 44.6 %collective-permute-start.16 = (bf16[2,160,2048]{2,1,0:T(8,128)(2,1)}, bf16[2,160,2048]{2,1,0:T(8,128)(2,1)}, u32[]{:S(2)}, u32[]{:S(2)}) collective-permute-start(bf16[2,160,2048]{2,1,0:T(8,128)(2,1)} %param.35), channel_id=1, source_target_pairs={{0,1},{1,0},{2,3},{3,2},{4,5},{5,4},{6,7},{7,6},{8,9},{9,8},{10,11... | collective-permute-start | bytes 3932168 | tf_op jit(solution)/shard_map/ppermute | solution.py:22
  187.1 51.2 %collective-permute-start.8 = (bf16[2,160,2048]{2,1,0:T(8,128)(2,1)S(1)}, bf16[2,160,2048]{2,1,0:T(8,128)(2,1)S(1)}, u32[]{:S(2)}, u32[]{:S(2)}) collective-permute-start(bf16[2,160,2048]{2,1,0:T(8,128)(2,1)S(1)} %get-tuple-element.46), channel_id=1, source_target_pairs={{0,1},{1,0},{2,3},{3,2},{4,5},{5,4},{6,7},{7,6},{8,9},{9,8},{10,11... | collective-permute-start | bytes 3932168 | tf_op jit(solution)/shard_map/ppermute | solution.py:22
  187.6 51.5 %collective-permute-start.9 = (bf16[2,160,2048]{2,1,0:T(8,128)(2,1)S(1)}, bf16[2,160,2048]{2,1,0:T(8,128)(2,1)S(1)}, u32[]{:S(2)}, u32[]{:S(2)}) collective-permute-start(bf16[2,160,2048]{2,1,0:T(8,128)(2,1)S(1)} %get-tuple-element.46), channel_id=1, source_target_pairs={{0,2},{1,3},{2,0},{3,1},{4,6},{5,7},{6,4},{7,5},{8,10},{9,11},{10,... | collective-permute-start | bytes 3932168 | tf_op jit(solution)/shard_map/ppermute | solution.py:23
  197.8 54.6 %collective-permute-start.18 = (bf16[2,80,2048]{2,1,0:T(8,128)(2,1)S(1)}, bf16[2,80,2048]{2,1,0:T(8,128)(2,1)S(1)}, u32[]{:S(2)}, u32[]{:S(2)}) collective-permute-start(bf16[2,80,2048]{2,1,0:T(8,128)(2,1)S(1)} %slice.108), channel_id=1, source_target_pairs={{0,1},{1,0},{2,3},{3,2},{4,5},{5,4},{6,7},{7,6},{8,9},{9,8},{10,11... | collective-permute-start | bytes 1966088 | tf_op jit(solution)/shard_map/ppermute | solution.py:24
  211.5 40.9 %collective-permute-start.19 = (bf16[2,80,2048]{2,1,0:T(8,128)(2,1)S(1)}, bf16[2,80,2048]{2,1,0:T(8,128)(2,1)S(1)}, u32[]{:S(2)}, u32[]{:S(2)}) collective-permute-start(bf16[2,80,2048]{2,1,0:T(8,128)(2,1)S(1)} %slice.109), channel_id=1, source_target_pairs={{0,2},{1,3},{2,0},{3,1},{4,6},{5,7},{6,4},{7,5},{8,10},{9,11},{10,... | collective-permute-start | bytes 1966088 | tf_op jit(solution)/shard_map/ppermute | solution.py:25
  238.4 16.6 %collective-permute-start.11 = (bf16[2,80,2048]{2,1,0:T(8,128)(2,1)S(1)}, bf16[2,80,2048]{2,1,0:T(8,128)(2,1)S(1)}, u32[]{:S(2)}, u32[]{:S(2)}) collective-permute-start(bf16[2,80,2048]{2,1,0:T(8,128)(2,1)S(1)} %slice.103), channel_id=1, source_target_pairs={{0,2},{1,3},{2,0},{3,1},{4,6},{5,7},{6,4},{7,5},{8,10},{9,11},{10,... | collective-permute-start | bytes 1966088 | tf_op jit(solution)/shard_map/ppermute | solution.py:25
  239.1 24.5 %collective-permute-start.10 = (bf16[2,80,2048]{2,1,0:T(8,128)(2,1)S(1)}, bf16[2,80,2048]{2,1,0:T(8,128)(2,1)S(1)}, u32[]{:S(2)}, u32[]{:S(2)}) collective-permute-start(bf16[2,80,2048]{2,1,0:T(8,128)(2,1)S(1)} %slice.102), channel_id=1, source_target_pairs={{0,1},{1,0},{2,3},{3,2},{4,5},{5,4},{6,7},{7,6},{8,9},{9,8},{10,11... | collective-permute-start | bytes 1966088 | tf_op jit(solution)/shard_map/ppermute | solution.py:24
  286.2 26.4 %copy-start.10 = (f32[2,640,2048]{2,1,0:T(8,128)}, f32[2,640,2048]{2,1,0:T(8,128)S(1)}, u32[]{:S(2)}) copy-start(f32[2,640,2048]{2,1,0:T(8,128)S(1)} %get-tuple-element.77) | copy-start | bytes 31457284
  355.2 21.2 %copy-start.11 = (f32[2,640,2048]{2,1,0:T(8,128)S(1)}, f32[2,640,2048]{2,1,0:T(8,128)}, u32[]{:S(2)}) copy-start(f32[2,640,2048]{2,1,0:T(8,128)} %fusion.10) | copy-start | bytes 31457284
  376.1 31.7 %collective-permute-start.20 = (bf16[2,2,80,2048]{3,2,1,0:T(8,128)(2,1)S(1)}, bf16[2,2,80,2048]{3,2,1,0:T(8,128)(2,1)S(1)}, u32[]{:S(2)}, u32[]{:S(2)}) collective-permute-start(bf16[2,2,80,2048]{3,2,1,0:T(8,128)(2,1)S(1)} %pad_maximum_fusion.6), channel_id=1, source_target_pairs={{0,1},{1,0},{2,3},{3,2},{4,5},{5,4},{6,7},{7,6},{8,9},{9,8},{10,11... | collective-permute-start | bytes 3932168 | tf_op jit(solution)/shard_map/ppermute | solution.py:53
  376.9 55.2 %collective-permute-start.12 = (bf16[2,2,80,2048]{3,2,1,0:T(8,128)(2,1)S(1)}, bf16[2,2,80,2048]{3,2,1,0:T(8,128)(2,1)S(1)}, u32[]{:S(2)}, u32[]{:S(2)}) collective-permute-start(bf16[2,2,80,2048]{3,2,1,0:T(8,128)(2,1)S(1)} %pad_maximum_fusion.4), channel_id=1, source_target_pairs={{0,1},{1,0},{2,3},{3,2},{4,5},{5,4},{6,7},{7,6},{8,9},{9,8},{10,11... | collective-permute-start | bytes 3932168 | tf_op jit(solution)/shard_map/ppermute | solution.py:53
  378.9 53.7 %collective-permute-start.22 = (bf16[2,2,80,2048]{3,2,1,0:T(8,128)(2,1)S(1)}, bf16[2,2,80,2048]{3,2,1,0:T(8,128)(2,1)S(1)}, u32[]{:S(2)}, u32[]{:S(2)}) collective-permute-start(bf16[2,2,80,2048]{3,2,1,0:T(8,128)(2,1)S(1)} %pad_maximum_fusion.7), channel_id=1, source_target_pairs={{0,2},{1,3},{2,0},{3,1},{4,6},{5,7},{6,4},{7,5},{8,10},{9,11},{10,... | collective-permute-start | bytes 3932168 | tf_op jit(solution)/shard_map/ppermute | solution.py:54
  379.5 76.4 %collective-permute-start.14 = (bf16[2,2,80,2048]{3,2,1,0:T(8,128)(2,1)S(1)}, bf16[2,2,80,2048]{3,2,1,0:T(8,128)(2,1)S(1)}, u32[]{:S(2)}, u32[]{:S(2)}) collective-permute-start(bf16[2,2,80,2048]{3,2,1,0:T(8,128)(2,1)S(1)} %pad_maximum_fusion.5), channel_id=1, source_target_pairs={{0,2},{1,3},{2,0},{3,1},{4,6},{5,7},{6,4},{7,5},{8,10},{9,11},{10,... | collective-permute-start | bytes 3932168 | tf_op jit(solution)/shard_map/ppermute | solution.py:54
  409.3 43.5 %collective-permute-start.21 = (bf16[2,80,2048]{2,1,0:T(8,128)(2,1)S(1)}, bf16[2,80,2048]{2,1,0:T(8,128)(2,1)S(1)}, u32[]{:S(2)}, u32[]{:S(2)}) collective-permute-start(bf16[2,80,2048]{2,1,0:T(8,128)(2,1)S(1)} %fusion.78), channel_id=1, source_target_pairs={{0,2},{1,3},{2,0},{3,1},{4,6},{5,7},{6,4},{7,5},{8,10},{9,11},{10,... | collective-permute-start | bytes 1966088 | tf_op jit(solution)/shard_map/ppermute | solution.py:57
  432.3 30.2 %collective-permute-start.13 = (bf16[2,80,2048]{2,1,0:T(8,128)(2,1)S(1)}, bf16[2,80,2048]{2,1,0:T(8,128)(2,1)S(1)}, u32[]{:S(2)}, u32[]{:S(2)}) collective-permute-start(bf16[2,80,2048]{2,1,0:T(8,128)(2,1)S(1)} %fusion.82), channel_id=1, source_target_pairs={{0,2},{1,3},{2,0},{3,1},{4,6},{5,7},{6,4},{7,5},{8,10},{9,11},{10,... | collective-permute-start | bytes 1966088 | tf_op jit(solution)/shard_map/ppermute | solution.py:57
  455.6 15.3 %collective-permute-start.23 = (bf16[2,80,2048]{2,1,0:T(8,128)(2,1)S(1)}, bf16[2,80,2048]{2,1,0:T(8,128)(2,1)S(1)}, u32[]{:S(2)}, u32[]{:S(2)}) collective-permute-start(bf16[2,80,2048]{2,1,0:T(8,128)(2,1)S(1)} %get-tuple-element.56), channel_id=1, source_target_pairs={{0,1},{1,0},{2,3},{3,2},{4,5},{5,4},{6,7},{7,6},{8,9},{9,8},{10,11... | collective-permute-start | bytes 1966088 | tf_op jit(solution)/shard_map/ppermute | solution.py:58
  463.0 17.2 %collective-permute-start.15 = (bf16[2,80,2048]{2,1,0:T(8,128)(2,1)S(1)}, bf16[2,80,2048]{2,1,0:T(8,128)(2,1)S(1)}, u32[]{:S(2)}, u32[]{:S(2)}) collective-permute-start(bf16[2,80,2048]{2,1,0:T(8,128)(2,1)S(1)} %get-tuple-element.62), channel_id=1, source_target_pairs={{0,1},{1,0},{2,3},{3,2},{4,5},{5,4},{6,7},{7,6},{8,9},{9,8},{10,11... | collective-permute-start | bytes 1966088 | tf_op jit(solution)/shard_map/ppermute | solution.py:58
  485.7 26.1 %collective-permute-start.24 = (bf16[2,160,2048]{2,1,0:T(8,128)(2,1)S(1)}, bf16[2,160,2048]{2,1,0:T(8,128)(2,1)S(1)}, u32[]{:S(2)}, u32[]{:S(2)}) collective-permute-start(bf16[2,160,2048]{2,1,0:T(8,128)(2,1)S(1)} %get-tuple-element.40), channel_id=1, source_target_pairs={{0,1},{1,0},{2,3},{3,2},{4,5},{5,4},{6,7},{7,6},{8,9},{9,8},{10,11... | collective-permute-start | bytes 3932168 | tf_op jit(solution)/shard_map/ppermute | solution.py:22
  486.1 27.6 %collective-permute-start.25 = (bf16[2,160,2048]{2,1,0:T(8,128)(2,1)S(1)}, bf16[2,160,2048]{2,1,0:T(8,128)(2,1)S(1)}, u32[]{:S(2)}, u32[]{:S(2)}) collective-permute-start(bf16[2,160,2048]{2,1,0:T(8,128)(2,1)S(1)} %get-tuple-element.40), channel_id=1, source_target_pairs={{0,2},{1,3},{2,0},{3,1},{4,6},{5,7},{6,4},{7,5},{8,10},{9,11},{10,... | collective-permute-start | bytes 3932168 | tf_op jit(solution)/shard_map/ppermute | solution.py:23
  512.9 22.6 %slice-start = ((s8[13107200]{0:T(1024)(128)(4,1)}), s8[524288]{0:T(1024)(128)(4,1)S(1)}, s32[]{:S(2)}) async-start(s8[13107200]{0:T(1024)(128)(4,1)} %bitcast.239), calls=%async_computation.18 | async-start | bytes 1048576
  513.0 13.1 %collective-permute-start.27 = (bf16[2,80,2048]{2,1,0:T(8,128)(2,1)S(1)}, bf16[2,80,2048]{2,1,0:T(8,128)(2,1)}, u32[]{:S(2)}, u32[]{:S(2)}) collective-permute-start(bf16[2,80,2048]{2,1,0:T(8,128)(2,1)S(1)} %slice.115), channel_id=1, source_target_pairs={{0,2},{1,3},{2,0},{3,1},{4,6},{5,7},{6,4},{7,5},{8,10},{9,11},{10,... | collective-permute-start | bytes 1966088 | tf_op jit(solution)/shard_map/ppermute | solution.py:25
  515.7 11.8 %collective-permute-start.26 = (bf16[2,80,2048]{2,1,0:T(8,128)(2,1)}, bf16[2,80,2048]{2,1,0:T(8,128)(2,1)}, u32[]{:S(2)}, u32[]{:S(2)}) collective-permute-start(bf16[2,80,2048]{2,1,0:T(8,128)(2,1)} %slice.114), channel_id=1, source_target_pairs={{0,1},{1,0},{2,3},{3,2},{4,5},{5,4},{6,7},{7,6},{8,9},{9,8},{10,11... | collective-permute-start | bytes 1966088 | tf_op jit(solution)/shard_map/ppermute | solution.py:24
  519.3 177.2 %reduce-scatter.30.cloned.1.call-start = ((), (), s32[]{:S(2)}) async-start(), calls=%async_computation.16 | async-start | bytes 36864
  545.5 152.4 %reduce-scatter.28.cloned.1.call-start = ((), (), s32[]{:S(2)}) async-start(), calls=%async_computation.15 | async-start | bytes 36864
  558.6 201.9 %reduce-scatter.22.cloned.1.call-start = ((), (), s32[]{:S(2)}) async-start(), calls=%async_computation.12 | async-start | bytes 2359296 | tf_op jit(solution)/shard_map/reduce_scatter | solution.py:228
  565.9 196.3 %reduce-scatter.20.cloned.1.call-start = ((), (), s32[]{:S(2)}) async-start(), calls=%async_computation.11 | async-start | bytes 2359296 | tf_op jit(solution)/shard_map/reduce_scatter | solution.py:219
  572.8 191.3 %reduce-scatter.16.cloned.1.call-start = ((), (), s32[]{:S(2)}) async-start(), calls=%async_computation.9 | async-start | bytes 2359296 | tf_op jit(solution)/shard_map/reduce_scatter | solution.py:213
  579.7 186.1 %reduce-scatter.18.cloned.1.call-start = ((), (), s32[]{:S(2)}) async-start(), calls=%async_computation.10 | async-start | bytes 2359296 | tf_op jit(solution)/shard_map/reduce_scatter | solution.py:216
  593.8 257.8 %reduce-scatter.24.cloned.1.call-start = ((), (), s32[]{:S(2)}) async-start(), calls=%async_computation.13 | async-start | bytes 9437184 | tf_op jit(solution)/shard_map/reduce_scatter | solution.py:231
  610.6 331.4 %reduce-scatter.26.cloned.1.call-start = ((), (), s32[]{:S(2)}) async-start(), calls=%async_computation.14 | async-start | bytes 9437184 | tf_op jit(solution)/shard_map/reduce_scatter | solution.py:234
  651.1 42.2 %copy-start.7 = (f32[2,640,2048]{2,1,0:T(8,128)}, f32[2,640,2048]{2,1,0:T(8,128)S(1)}, u32[]{:S(2)}) copy-start(f32[2,640,2048]{2,1,0:T(8,128)S(1)} %add_add_fusion) | copy-start | bytes 31457284
  651.6 26.0 %collective-permute-start.28 = (bf16[2,2,80,2048]{3,2,1,0:T(8,128)(2,1)S(1)}, bf16[2,2,80,2048]{3,2,1,0:T(8,128)(2,1)S(1)}, u32[]{:S(2)}, u32[]{:S(2)}) collective-permute-start(bf16[2,2,80,2048]{3,2,1,0:T(8,128)(2,1)S(1)} %pad_maximum_fusion.8), channel_id=1, source_target_pairs={{0,1},{1,0},{2,3},{3,2},{4,5},{5,4},{6,7},{7,6},{8,9},{9,8},{10,11... | collective-permute-start | bytes 3932168 | tf_op jit(solution)/shard_map/ppermute | solution.py:53
  653.8 29.8 %collective-permute-start.30 = (bf16[2,2,80,2048]{3,2,1,0:T(8,128)(2,1)S(1)}, bf16[2,2,80,2048]{3,2,1,0:T(8,128)(2,1)S(1)}, u32[]{:S(2)}, u32[]{:S(2)}) collective-permute-start(bf16[2,2,80,2048]{3,2,1,0:T(8,128)(2,1)S(1)} %pad_maximum_fusion.9), channel_id=1, source_target_pairs={{0,2},{1,3},{2,0},{3,1},{4,6},{5,7},{6,4},{7,5},{8,10},{9,11},{10,... | collective-permute-start | bytes 3932168 | tf_op jit(solution)/shard_map/ppermute | solution.py:54
  677.8 15.5 %collective-permute-start.29 = (bf16[2,80,2048]{2,1,0:T(8,128)(2,1)S(1)}, bf16[2,80,2048]{2,1,0:T(8,128)(2,1)S(1)}, u32[]{:S(2)}, u32[]{:S(2)}) collective-permute-start(bf16[2,80,2048]{2,1,0:T(8,128)(2,1)S(1)} %fusion.74), channel_id=1, source_target_pairs={{0,2},{1,3},{2,0},{3,1},{4,6},{5,7},{6,4},{7,5},{8,10},{9,11},{10,... | collective-permute-start | bytes 1966088 | tf_op jit(solution)/shard_map/ppermute | solution.py:57
  694.7 12.7 %collective-permute-start.31 = (bf16[2,80,2048]{2,1,0:T(8,128)(2,1)}, bf16[2,80,2048]{2,1,0:T(8,128)(2,1)S(1)}, u32[]{:S(2)}, u32[]{:S(2)}) collective-permute-start(bf16[2,80,2048]{2,1,0:T(8,128)(2,1)} %get-tuple-element.51), channel_id=1, source_target_pairs={{0,1},{1,0},{2,3},{3,2},{4,5},{5,4},{6,7},{7,6},{8,9},{9,8},{10,11... | collective-permute-start | bytes 1966088 | tf_op jit(solution)/shard_map/ppermute | solution.py:58
  765.8 178.8 %copy-start.1 = (bf16[512,2048]{1,0:T(8,128)(2,1)S(1)}, bf16[512,2048]{1,0:T(8,128)(2,1)}, u32[]{:S(2)}) copy-start(bf16[512,2048]{1,0:T(8,128)(2,1)} %param.25) | copy-start | bytes 6291460
  (58 other events, 343.3 us)
Sparse Core Ops, SparseCore 0:
  519.4 29.9 reduce-scatter.31
  552.2 28.6 reduce-scatter.29
  583.7 28.6 reduce-scatter.27
  614.6 34.1 reduce-scatter.21
  651.0 34.6 reduce-scatter.19
  688.4 34.5 reduce-scatter.15
  725.8 34.7 reduce-scatter.17
  762.9 88.7 reduce-scatter.23
  853.9 87.9 reduce-scatter.25
